TPU v7x, 256 devices: a whole 4x4x8 slice. The times are simulated.
256 devices in a mesh: rep: 4 (over x), gx: 8 (over z), gy: 8 (over y, core).
Axes of the slice: x: 4, y: 4, z: 8, core: 2. Of those that a mesh axis runs over, the one named last changes fastest.
Arguments:
- features: bfloat16 [4, 8, 8, 512, 128], P('rep', 'gx', 'gy'), may hold values from -6 to 6
- species: int32 [4, 8, 8, 512], P('rep', 'gx', 'gy'), may hold values from 0 to 2
- atom_nbr: int32 [4, 8, 8, 512, 32], P('rep', 'gx', 'gy'), may hold values from 0 to 1535, as said below
- atom_nbr_count: int32 [4, 8, 8, 512], P('rep', 'gx', 'gy'), may hold values from 16 to 32
- atom_dist: float32 [4, 8, 8, 512, 32], P('rep', 'gx', 'gy'), may hold values from 0.8 to 3.9
- send_list: int32 [4, 8, 8, 8, 128], P('rep', 'gx', 'gy'), may hold values from 0 to 511
- probe_nbr: int32 [4, 8, 8, 1024, 32], P('rep', 'gx', 'gy'), may hold values from 0 to 1535, as said below
- probe_dist: float32 [4, 8, 8, 1024, 32], P('rep', 'gx', 'gy'), may hold values from 0.3 to 3.9
- probe_count: int32 [4, 8, 8], P('rep', 'gx', 'gy'), may hold values from 128 to 1024, as said below
- d_density: float32 [4, 8, 8, 1024], P('rep', 'gx', 'gy'), may hold values from -0.03 to 0.03
- species_gain: float32 [3, 128], replicated, may hold values from 0.1 to 1.9
- proj_input: bfloat16 [128, 128], replicated, may hold values from -0.5 to 0.5
- atom_radial: bfloat16 [20, 128], replicated, may hold values from -4 to 4
- atom_filter: bfloat16 [128, 128], replicated, may hold values from -0.5 to 0.5
- mix_first: bfloat16 [128, 128], replicated, may hold values from -0.5 to 0.5
- mix_second: bfloat16 [128, 128], replicated, may hold values from -0.5 to 0.5
- proj_probe: bfloat16 [128, 128], replicated, may hold values from -0.5 to 0.5
- probe_radial: bfloat16 [20, 128], replicated, may hold values from -4 to 4
- probe_filter: bfloat16 [128, 128], replicated, may hold values from -0.5 to 0.5
- read_weight: bfloat16 [128, 128], replicated, may hold values from -0.5 to 0.5
- final_weight: float32 [128], replicated, may hold values from -0.5 to 0.5
Outputs:
- d_features: float32 [4, 8, 8, 512, 128], P('rep', 'gx', 'gy')
- grad_square: float32 [7, 128, 128], replicated
- grad_radial: float32 [2, 20, 128], replicated
- grad_vector: float32 [4, 128], replicated
Inputs may be any that keep to these rules, and one draw needn't show every extreme that they name: `atom_nbr`: entries below 512 name the tile's own atoms; entry 512 + k * 128 + g names row g of ghost block k. About a quarter of the entries name ghost rows. `probe_nbr`: same layout as atom_nbr. About a quarter of the entries name ghost rows. `probe_count`: equal to 1024 on at least one tile of every draw.
All inputs are finite; a program needn't handle non-finite values.
Results may differ from a plain program's by a relative error of at most 0.014.
Values may be sent and summed in bfloat16 or wider, within the bound.
No kernel may reach another device: no remote copies, remote signals or barrier semaphores. Data moves between devices by JAX's collectives and lax.ppermute only.
A program may use at most 64 MiB of HBM per device.

v0:
```python
import math
import jax
import jax.numpy as jnp
from jax import lax
from jax.sharding import PartitionSpec as P

cutoff_radius = 4.0


def with_halo(block, sides, width):
    for axis, dim in sides:
        count = lax.axis_size(axis)
        forward = [(i, i + 1) for i in range(count - 1)]
        forward.append((count - 1, 0))
        backward = [(target, source) for source, target in forward]
        low = lax.ppermute(
            lax.slice_in_dim(block, block.shape[dim] - width, None, axis=dim), axis, forward
        )
        high = lax.ppermute(lax.slice_in_dim(block, 0, width, axis=dim), axis, backward)
        block = jnp.concatenate([low, block, high], axis=dim)
    return block


def shifted_plus(values):
    return jax.nn.softplus(values) - math.log(2.0)


def contract_rows(former, latter):
    return lax.dot_general(
        former, latter, (((0,), (0,)), ((), ())), preferred_element_type=jnp.float32
    )


def contract_cols(former, latter):
    return lax.dot_general(
        former, latter, (((1,), (1,)), ((), ())), preferred_element_type=jnp.float32
    )


def edge_setup(indices, distances, live_mask, row_table, radial_weight, filter_weight):
    flat_dist = distances.reshape(-1)
    spacing = cutoff_radius / (radial_weight.shape[0] - 1)
    centers = jnp.arange(radial_weight.shape[0], dtype=jnp.float32) * spacing
    scaled = (flat_dist[None, :] - centers[:, None]) / spacing
    expansion = jnp.exp(-scaled * scaled).astype(jnp.bfloat16)
    pre_act = contract_rows(expansion, radial_weight)
    hidden = shifted_plus(pre_act).astype(jnp.bfloat16)
    envelope = 0.5 * (jnp.cos(math.pi * flat_dist / cutoff_radius) + 1.0) * live_mask.reshape(-1)
    filters = jnp.dot(hidden, filter_weight, preferred_element_type=jnp.float32) * envelope[:, None]
    gathered = row_table[indices.reshape(-1)].astype(jnp.float32)
    return (expansion, pre_act, hidden, envelope, filters, gathered)


def edge_sums(stored, slot_count):
    filters = stored[4]
    gathered = stored[5]
    terms = (gathered * filters).reshape(-1, slot_count, filters.shape[1])
    return jnp.sum(terms, axis=1)


def edge_backward(stored, indices, filter_weight, grad_message, totals):
    expansion, pre_act, hidden, envelope, filters, gathered = stored
    grad_table, grad_radial, grad_filter = totals
    feature_width = grad_message.shape[1]
    spread = jnp.broadcast_to(
        grad_message[:, None, :], (grad_message.shape[0], indices.shape[1], feature_width)
    ).reshape(-1, feature_width)
    grad_table = grad_table.at[indices.reshape(-1)].add(spread * filters)
    grad_out = (spread * gathered * envelope[:, None]).astype(jnp.bfloat16)
    grad_filter = grad_filter + contract_rows(hidden, grad_out)
    grad_pre = (contract_cols(grad_out, filter_weight) * jax.nn.sigmoid(pre_act)).astype(
        jnp.bfloat16
    )
    grad_radial = grad_radial + jnp.dot(expansion, grad_pre, preferred_element_type=jnp.float32)
    return (grad_table, grad_radial, grad_filter)


def slot_mask(counts, slot_count):
    return (jnp.arange(slot_count, dtype=jnp.int32)[None, :] < counts[:, None]).astype(jnp.float32)


def atom_messages(indices, distances, counts, row_table, radial_weight, filter_weight):
    atom_count, slot_count = indices.shape
    block_rows = min(64, atom_count)
    pieces = (
        indices.reshape(-1, block_rows, slot_count),
        distances.reshape(-1, block_rows, slot_count),
        slot_mask(counts, slot_count).reshape(-1, block_rows, slot_count),
    )

    def one_block(portion):
        stored = edge_setup(
            portion[0], portion[1], portion[2], row_table, radial_weight, filter_weight
        )
        return edge_sums(stored, slot_count)

    return lax.map(one_block, pieces).reshape(atom_count, -1)


def atom_backward(
    indices, distances, counts, row_table, radial_weight, filter_weight, grad_message
):
    atom_count, slot_count = indices.shape
    block_rows = min(64, atom_count)
    pieces = (
        indices.reshape(-1, block_rows, slot_count),
        distances.reshape(-1, block_rows, slot_count),
        slot_mask(counts, slot_count).reshape(-1, block_rows, slot_count),
        grad_message.reshape(-1, block_rows, grad_message.shape[1]),
    )
    initial = (
        jnp.zeros(row_table.shape, jnp.float32),
        jnp.zeros(radial_weight.shape, jnp.float32),
        jnp.zeros(filter_weight.shape, jnp.float32),
    )

    def advance(totals, portion):
        stored = edge_setup(
            portion[0], portion[1], portion[2], row_table, radial_weight, filter_weight
        )
        return (edge_backward(stored, portion[0], filter_weight, portion[3], totals), None)

    return lax.scan(advance, initial, pieces)[0]


def probe_block(
    totals,
    indices,
    distances,
    cotangent,
    row_table,
    probe_radial,
    probe_filter,
    read_weight,
    final_weight,
):
    grad_table, grad_radial, grad_filter, grad_read, grad_final = totals
    stored = edge_setup(
        indices,
        distances,
        jnp.ones(indices.shape, jnp.float32),
        row_table,
        probe_radial,
        probe_filter,
    )
    packed = edge_sums(stored, indices.shape[1]).astype(jnp.bfloat16)
    read_pre = jnp.dot(packed, read_weight, preferred_element_type=jnp.float32)
    grad_final = grad_final + jnp.sum(cotangent[:, None] * shifted_plus(read_pre), axis=0)
    grad_inner = (cotangent[:, None] * final_weight[None, :] * jax.nn.sigmoid(read_pre)).astype(
        jnp.bfloat16
    )
    grad_read = grad_read + contract_rows(packed, grad_inner)
    grad_feats = contract_cols(grad_inner, read_weight)
    edge_totals = edge_backward(
        stored, indices, probe_filter, grad_feats, (grad_table, grad_radial, grad_filter)
    )
    return edge_totals + (grad_read, grad_final)


def interaction_head(atom_feats, kinds, species_gain, proj_input):
    onehot = (kinds[:, None] == jnp.arange(species_gain.shape[0], dtype=jnp.int32)[None, :]).astype(
        jnp.float32
    )
    gains = jnp.dot(onehot, species_gain, precision=lax.Precision.HIGHEST)
    scaled = (atom_feats.astype(jnp.float32) * gains).astype(jnp.bfloat16)
    projected = jnp.dot(scaled, proj_input, preferred_element_type=jnp.float32).astype(jnp.bfloat16)
    return (onehot, gains, scaled, projected)


def interaction_tail(atom_feats, message, mix_first, mix_second, proj_probe):
    packed_msg = message.astype(jnp.bfloat16)
    mix_pre = jnp.dot(packed_msg, mix_first, preferred_element_type=jnp.float32)
    activation = shifted_plus(mix_pre).astype(jnp.bfloat16)
    updated = (
        atom_feats.astype(jnp.float32)
        + jnp.dot(activation, mix_second, preferred_element_type=jnp.float32)
    ).astype(jnp.bfloat16)
    probe_proj = jnp.dot(updated, proj_probe, preferred_element_type=jnp.float32).astype(
        jnp.bfloat16
    )
    return (packed_msg, mix_pre, activation, updated, probe_proj)


def tail_backward(
    grad_proj, packed_msg, mix_pre, activation, updated, mix_first, mix_second, proj_probe
):
    grad_packed = grad_proj.astype(jnp.bfloat16)
    grad_proj_probe = contract_rows(updated, grad_packed)
    grad_updated = contract_cols(grad_packed, proj_probe)
    grad_upd_packed = grad_updated.astype(jnp.bfloat16)
    grad_mix_second = contract_rows(activation, grad_upd_packed)
    grad_mix_pre = (contract_cols(grad_upd_packed, mix_second) * jax.nn.sigmoid(mix_pre)).astype(
        jnp.bfloat16
    )
    grad_mix_first = contract_rows(packed_msg, grad_mix_pre)
    grad_message = contract_cols(grad_mix_pre, mix_first)
    return (grad_updated, grad_message, grad_proj_probe, grad_mix_second, grad_mix_first)


def head_backward(grad_proj, grad_updated, atom_feats, onehot, gains, scaled, proj_input):
    grad_packed = grad_proj.astype(jnp.bfloat16)
    grad_proj_input = contract_rows(scaled, grad_packed)
    grad_scaled = contract_cols(grad_packed, proj_input)
    d_features = grad_updated + grad_scaled * gains
    grad_gain = lax.dot_general(
        onehot,
        grad_scaled * atom_feats.astype(jnp.float32),
        (((0,), (0,)), ((), ())),
        precision=lax.Precision.HIGHEST,
    )
    return (d_features, grad_proj_input, grad_gain)


def add_rows(base, send_rows, returned):
    return base.at[send_rows.reshape(-1)].add(returned.reshape(-1, returned.shape[-1]))


def grid_of(blocks):
    empty = jnp.zeros((1,) + blocks.shape[1:], blocks.dtype)
    return jnp.concatenate([blocks[:4], empty, blocks[4:]], axis=0).reshape(
        (3, 3) + blocks.shape[1:]
    )


def blocks_of(layout):
    flat_grid = layout.reshape((9,) + layout.shape[2:])
    return jnp.concatenate([flat_grid[:4], flat_grid[5:]], axis=0)


def ghost_rows(blocks):
    layout = grid_of(blocks)
    padded = with_halo(layout, (("gx", 0), ("gy", 1)), 1)
    arrived = padded[0::2, 0::2]
    return blocks_of(arrived)


def ghost_grads(blocks):
    layout = grid_of(blocks)
    padded = with_halo(layout.astype(jnp.bfloat16), (("gx", 0), ("gy", 1)), 1).astype(layout.dtype)
    arrived = padded[0::2, 0::2]
    return blocks_of(arrived)


def per_device(
    features,
    species,
    atom_nbr,
    atom_nbr_count,
    atom_dist,
    send_list,
    probe_nbr,
    probe_dist,
    probe_count,
    d_density,
    species_gain,
    proj_input,
    atom_radial,
    atom_filter,
    mix_first,
    mix_second,
    proj_probe,
    probe_radial,
    probe_filter,
    read_weight,
    final_weight,
):
    atom_feats = features[0, 0, 0]
    atom_count = atom_feats.shape[0]
    feature_width = atom_feats.shape[1]
    send_rows = send_list[0, 0, 0]
    tile_nbr = atom_nbr[0, 0, 0]
    tile_dist = atom_dist[0, 0, 0]
    tile_counts = atom_nbr_count[0, 0, 0]
    onehot, gains, scaled, projected = interaction_head(
        atom_feats, species[0, 0, 0], species_gain, proj_input
    )
    row_table = jnp.concatenate(
        [projected, ghost_rows(projected[send_rows]).reshape(-1, feature_width)], axis=0
    )
    message = atom_messages(tile_nbr, tile_dist, tile_counts, row_table, atom_radial, atom_filter)
    packed_msg, mix_pre, activation, updated, probe_proj = interaction_tail(
        atom_feats, message, mix_first, mix_second, proj_probe
    )
    probe_table = jnp.concatenate(
        [probe_proj, ghost_rows(probe_proj[send_rows]).reshape(-1, feature_width)], axis=0
    )
    probe_ids = probe_nbr[0, 0, 0]
    probe_far = probe_dist[0, 0, 0]
    cotangents = d_density[0, 0, 0]
    block_rows = min(64, probe_ids.shape[0])
    active = probe_count[0, 0, 0]
    turns = (active + block_rows - 1) // block_rows
    initial = (
        jnp.zeros(probe_table.shape, jnp.float32),
        jnp.zeros(probe_radial.shape, jnp.float32),
        jnp.zeros(probe_filter.shape, jnp.float32),
        jnp.zeros(read_weight.shape, jnp.float32),
        jnp.zeros(final_weight.shape, jnp.float32),
    )

    def probe_turn(turn_index, totals):
        first_row = turn_index * block_rows
        indices = lax.dynamic_slice_in_dim(probe_ids, first_row, block_rows, 0)
        distances = lax.dynamic_slice_in_dim(probe_far, first_row, block_rows, 0)
        positions = first_row + jnp.arange(block_rows, dtype=jnp.int32)
        cotangent = lax.dynamic_slice_in_dim(cotangents, first_row, block_rows, 0) * (
            positions < active
        ).astype(jnp.float32)
        return probe_block(
            totals,
            indices,
            distances,
            cotangent,
            probe_table,
            probe_radial,
            probe_filter,
            read_weight,
            final_weight,
        )

    grad_ptable, grad_pradial, grad_pfilter, grad_read, grad_final = lax.fori_loop(
        0, turns, probe_turn, initial
    )
    returned_probe = ghost_grads(
        grad_ptable[atom_count:].reshape(send_rows.shape + (feature_width,))
    )
    grad_q = add_rows(grad_ptable[:atom_count], send_rows, returned_probe)
    grad_updated, grad_message, grad_proj_probe, grad_mix_second, grad_mix_first = tail_backward(
        grad_q, packed_msg, mix_pre, activation, updated, mix_first, mix_second, proj_probe
    )
    grad_atable, grad_aradial, grad_afilter = atom_backward(
        tile_nbr, tile_dist, tile_counts, row_table, atom_radial, atom_filter, grad_message
    )
    returned_atom = ghost_grads(
        grad_atable[atom_count:].reshape(send_rows.shape + (feature_width,))
    )
    grad_u = add_rows(grad_atable[:atom_count], send_rows, returned_atom)
    d_features, grad_proj_input, grad_gain = head_backward(
        grad_u, grad_updated, atom_feats, onehot, gains, scaled, proj_input
    )
    (
        grad_pradial,
        grad_pfilter,
        grad_read,
        grad_final,
        grad_aradial,
        grad_afilter,
        grad_proj_input,
        grad_mix_first,
        grad_mix_second,
        grad_proj_probe,
        grad_gain,
    ) = lax.psum(
        (
            grad_pradial,
            grad_pfilter,
            grad_read,
            grad_final,
            grad_aradial,
            grad_afilter,
            grad_proj_input,
            grad_mix_first,
            grad_mix_second,
            grad_proj_probe,
            grad_gain,
        ),
        ("rep", "gx", "gy"),
    )
    grad_square = jnp.stack(
        [
            grad_pfilter,
            grad_read,
            grad_afilter,
            grad_proj_input,
            grad_mix_first,
            grad_mix_second,
            grad_proj_probe,
        ],
        axis=0,
    )
    grad_radial = jnp.stack([grad_pradial, grad_aradial], axis=0)
    grad_vector = jnp.concatenate([grad_final[None, :], grad_gain], axis=0)
    return (d_features[None, None, None], grad_square, grad_radial, grad_vector)


def solution(mesh):
    in_specs = (
        P("rep", "gx", "gy", None, None),
        P("rep", "gx", "gy", None),
        P("rep", "gx", "gy", None, None),
        P("rep", "gx", "gy", None),
        P("rep", "gx", "gy", None, None),
        P("rep", "gx", "gy", None, None),
        P("rep", "gx", "gy", None, None),
        P("rep", "gx", "gy", None, None),
        P("rep", "gx", "gy"),
        P("rep", "gx", "gy", None),
        P(),
        P(),
        P(),
        P(),
        P(),
        P(),
        P(),
        P(),
        P(),
        P(),
        P(),
    )
    out_specs = (P("rep", "gx", "gy", None, None), P(), P(), P())
    return jax.shard_map(
        per_device, mesh=mesh, in_specs=in_specs, out_specs=out_specs, check_vma=False
    )
```

profile of v0, /device:TPU:1, one launch (start us, length us, event | category | flops | bytes accessed | tf_op | source)
XLA Modules:
  0.0 1231.6 jit_solution(3619907784118653418)
XLA Ops:
  9.2 3.2 gather_fusion.3
  12.4 2.5 collective-permute-start
  15.0 4.0 collective-permute-start.1
  29.6 67.8 %while.50 = (s32[]{:T(128)}, bf16[8,64,128]{2,1,0:T(8,128)(2,1)S(1)}, s32[8,64,32]{2,1,0:T(8,128)S(1)}, bf16[1536,128]{1,0:T(8,128)(2,1)S(1)}, f32[8,64,32]{2,1,...) while((s32[]{:T(128)}, ...), condition=%wide.region_2.3_spmd, body=%wide.region_0.2_spmd.sunk | while | flops 80953368 | bytes 1840393 | solution.py:97
  30.7 6.2 gather_fusion
  39.2 6.2 gather_fusion
  47.7 6.2 gather_fusion
  56.2 6.2 gather_fusion
  64.6 6.2 gather_fusion
  73.1 6.2 gather_fusion
  81.6 6.2 gather_fusion
  90.1 6.2 gather_fusion
  99.8 3.2 gather_fusion.4
  103.1 2.9 collective-permute-start.5
  106.1 2.8 collective-permute-done.4
  117.1 99.2 %while.51 = (s32[]{:T(128)}, f32[1536,128]{1,0:T(8,128)S(1)}, f32[20,128]{1,0:T(8,128)}, f32[128,128]{1,0:T(8,128)}, f32[128,128]{1,0:T(8,128)}, /*index=5*/f32[...) while((s32[]{:T(128)}, f32[1536,128]{1,0:T(8,128)S(1)}, ...), condition=%wide.region_7.8_spmd, body=%wide.region_3.7_spmd.sunk | while | flops 237339360 | bytes 26602296 | solution.py:321
  119.8 6.2 gather_fusion.1
  136.4 11.8 scatter_fusion
  152.9 6.2 gather_fusion.1
  169.5 11.8 scatter_fusion
  185.9 6.2 gather_fusion.1
  202.6 11.8 scatter_fusion
  216.4 35.9 %collective-permute-start.8 = (bf16[1,3,128,128]{3,2,1,0:T(8,128)(2,1)S(1)}, bf16[1,3,128,128]{3,2,1,0:T(8,128)(2,1)S(1)}, u32[]{:S(2)}, u32[]{:S(2)}) collective-permute-start(bf16[1,3,128,128]{3,2,1,0:T(8,128)(2,1)S(1)} %bitcast.226), channel_id=1, source_target_pairs={{0,8},{8,16},{16,24},{24,32},{32,40},{40,48},{48,56},{56,0},{1,9},... | collective-permute-start | bytes 294920 | tf_op jit(solution)/shard_map/ppermute | solution.py:16
  252.3 66.7 %collective-permute-start.9 = (bf16[1,3,128,128]{3,2,1,0:T(8,128)(2,1)S(1)}, bf16[1,3,128,128]{3,2,1,0:T(8,128)(2,1)S(1)}, u32[]{:S(2)}, u32[]{:S(2)}) collective-permute-start(bf16[1,3,128,128]{3,2,1,0:T(8,128)(2,1)S(1)} %bitcast.224), channel_id=1, source_target_pairs={{8,0},{16,8},{24,16},{32,24},{40,32},{48,40},{56,48},{0,56},{9,1},... | collective-permute-start | bytes 294920 | tf_op jit(solution)/shard_map/ppermute | solution.py:19
  322.5 331.3 %collective-permute-start.10 = (bf16[5,1,128,128]{3,2,1,0:T(8,128)(2,1)S(1)}, bf16[5,1,128,128]{3,2,1,0:T(8,128)(2,1)S(1)}, u32[]{:S(2)}, u32[]{:S(2)}) collective-permute-start(bf16[5,1,128,128]{3,2,1,0:T(8,128)(2,1)S(1)} %get-tuple-element.638), channel_id=1, source_target_pairs={{0,1},{1,2},{2,3},{3,4},{4,5},{5,6},{6,7},{7,0},{8,9},{9,10},{10,1... | collective-permute-start | bytes 491528 | tf_op jit(solution)/shard_map/ppermute | solution.py:16
  656.1 2.8 collective-permute-done.11
  659.2 6.4 scatter_fusion.2
  669.0 197.2 %while.52 = (s32[]{:T(128)}, f32[1536,128]{1,0:T(8,128)S(1)}, f32[20,128]{1,0:T(8,128)S(1)}, f32[128,128]{1,0:T(8,128)}, s32[8,64,32]{2,1,0:T(8,128)}, /*index=5...) while((s32[]{:T(128)}, f32[1536,128]{1,0:T(8,128)S(1)}, ...), condition=%wide.region_11.12_spmd.clone, body=%wide.region_9.11_spmd.clone.sunk | while | flops 230102048 | bytes 15238644 | solution.py:123
  673.0 11.8 scatter_fusion.1
  684.8 6.2 gather_fusion.2
  697.7 11.8 scatter_fusion.1
  709.5 6.2 gather_fusion.2
  722.3 11.8 scatter_fusion.1
  734.1 6.2 gather_fusion.2
  746.9 11.8 scatter_fusion.1
  758.7 6.2 gather_fusion.2
  771.6 11.8 scatter_fusion.1
  783.4 6.2 gather_fusion.2
  796.2 11.8 scatter_fusion.1
  808.0 6.2 gather_fusion.2
  820.9 11.8 scatter_fusion.1
  832.7 6.2 gather_fusion.2
  845.5 11.8 scatter_fusion.1
  857.3 6.2 gather_fusion.2
  866.4 2.7 collective-permute-start.13
  878.3 6.1 scatter_fusion.3
  887.4 80.2 %all-reduce = (f32[1,20,128]{2,1,0:T(8,128)S(1)}, f32[1,20,128]{2,1,0:T(8,128)S(1)}, f32[3,128]{1,0:T(4,128)S(1)}, f32[1,128]{1,0:T(1,128)S(1)}) all-reduce(f32[1,20,128]{2,1,0:T(8,128)S(1)} %bitcast.232, f32[1,20,128]{2,1,0:T(8,128)S(1)} %bitcast.228, ...), channel_id=1, replica_groups=mesh['rep'=4,'gx'=8,'gy'=8] {'rep','gx','gy'}, use_global_device_ids=true, to_apply=%region_21.22 | all-reduce | flops 5632 | bytes 45056 | tf_op jit(solution)/shard_map/psum | solution.py:353
  969.7 249.2 %all-reduce.4.cloned.1.call-done = (f32[1,128,128]{2,1,0:T(8,128)}, f32[1,128,128]{2,1,0:T(8,128)}, f32[1,128,128]{2,1,0:T(8,128)}, f32[1,128,128]{2,1,0:T(8,128...) async-done(((f32[1,128,128]{2,1,0:T(8,128)}, f32[1,128,128]{2,1,0:T(8,128)}, f32[1,128,128]{2,1,0:T(8,128)}, f32[1,128,128]{2,1,0:T(8,128)}, ...) | async-done | bytes 458768 | tf_op jit(solution)/shard_map/psum | solution.py:353
  (642 shorter events, 167.0 us)
Async XLA Ops:
  7.2 92.4 %copy-start = (bf16[128,128]{1,0:T(8,128)(2,1)S(1)}, bf16[128,128]{1,0:T(8,128)(2,1)}, u32[]{:S(2)}) copy-start(bf16[128,128]{1,0:T(8,128)(2,1)} %param.43) | copy-start | bytes 98308
  7.2 1211.7 %all-reduce.4.cloned.1.call-start = ((), (), s32[]{:S(2)}) async-start(), calls=%async_computation | async-start | bytes 917504 | tf_op jit(solution)/shard_map/psum | solution.py:353
  12.4 9.2 collective-permute-start
  15.0 6.7 collective-permute-start.1
  19.1 87.0 %copy-start.59 = (bf16[9]{0:T(256)(128)(2,1)}, bf16[9]{0:T(256)(128)(2,1)S(1)}, u32[]{:S(2)}) copy-start(bf16[9]{0:T(256)(128)(2,1)S(1)} %pad.58.clone) | copy-start | bytes 58
  19.1 1.5 copy-start.39
  21.7 4.5 collective-permute-start.2
  23.9 4.7 collective-permute-start.3
  29.6 67.8 %copy-start.37 = (bf16[128,128]{1,0:T(8,128)(2,1)S(1)}, bf16[128,128]{1,0:T(8,128)(2,1)}, u32[]{:S(2)}) copy-start(bf16[128,128]{1,0:T(8,128)(2,1)} %param.41) | copy-start | bytes 98308
  103.0 5.9 collective-permute-start.4
  103.1 5.9 collective-permute-start.5
  109.0 1.5 copy-start.33
  109.0 3.5 collective-permute-start.6
  109.2 5.0 collective-permute-start.7
  118.8 7.2 copy-start.3
  129.0 1.6 copy-start.24
  132.2 1.7 copy-start.5
  133.8 2.6 copy-start.23
  136.4 11.8 copy-start.50
  151.9 7.2 copy-start.3
  162.1 1.6 copy-start.24
  165.2 1.7 copy-start.5
  166.9 2.6 copy-start.23
  169.5 11.8 copy-start.50
  185.0 7.2 copy-start.3
  195.2 1.6 copy-start.24
  198.3 1.7 copy-start.5
  200.0 2.6 copy-start.23
  202.6 11.8 copy-start.50
  216.4 104.5 %collective-permute-start.8 = (bf16[1,3,128,128]{3,2,1,0:T(8,128)(2,1)S(1)}, bf16[1,3,128,128]{3,2,1,0:T(8,128)(2,1)S(1)}, u32[]{:S(2)}, u32[]{:S(2)}) collective-permute-start(bf16[1,3,128,128]{3,2,1,0:T(8,128)(2,1)S(1)} %bitcast.226), channel_id=1, source_target_pairs={{0,8},{8,16},{16,24},{24,32},{32,40},{40,48},{48,56},{56,0},{1,9},... | collective-permute-start | bytes 294920 | tf_op jit(solution)/shard_map/ppermute | solution.py:16
  252.3 70.2 %collective-permute-start.9 = (bf16[1,3,128,128]{3,2,1,0:T(8,128)(2,1)S(1)}, bf16[1,3,128,128]{3,2,1,0:T(8,128)(2,1)S(1)}, u32[]{:S(2)}, u32[]{:S(2)}) collective-permute-start(bf16[1,3,128,128]{3,2,1,0:T(8,128)(2,1)S(1)} %bitcast.224), channel_id=1, source_target_pairs={{8,0},{16,8},{24,16},{32,24},{40,32},{48,40},{56,48},{0,56},{9,1},... | collective-permute-start | bytes 294920 | tf_op jit(solution)/shard_map/ppermute | solution.py:19
  322.5 331.4 %copy-start.52 = (s32[1,1,1,8,128]{4,3,2,1,0:T(8,128)S(1)}, s32[1,1,1,8,128]{4,3,2,1,0:T(8,128)}, u32[]{:S(2)}) copy-start(s32[1,1,1,8,128]{4,3,2,1,0:T(8,128)} %param.32) | copy-start | bytes 12292
  322.5 333.6 %collective-permute-start.10 = (bf16[5,1,128,128]{3,2,1,0:T(8,128)(2,1)S(1)}, bf16[5,1,128,128]{3,2,1,0:T(8,128)(2,1)S(1)}, u32[]{:S(2)}, u32[]{:S(2)}) collective-permute-start(bf16[5,1,128,128]{3,2,1,0:T(8,128)(2,1)S(1)} %get-tuple-element.638), channel_id=1, source_target_pairs={{0,1},{1,2},{2,3},{3,4},{4,5},{5,6},{6,7},{7,0},{8,9},{9,10},{10,1... | collective-permute-start | bytes 491528 | tf_op jit(solution)/shard_map/ppermute | solution.py:16
  653.8 5.0 collective-permute-start.11
  692.2 1.4 copy-start.10
  741.5 1.4 copy-start.10
  766.1 1.4 copy-start.10
  790.8 1.4 copy-start.10
  815.4 1.4 copy-start.10
  840.1 1.4 copy-start.10
  864.7 1.4 copy-start.10
  866.3 4.8 collective-permute-start.12
  866.4 4.7 collective-permute-start.13
  871.0 2.2 copy-start.19
  871.0 2.2 copy-start.21
  871.1 5.0 collective-permute-start.14
  872.9 5.0 collective-permute-start.15
  878.3 6.2 copy-start.36
  (100 other events, 85.5 us)
Sparse Core Ops, SparseCore 0:
  969.0 249.7 all-reduce.3
where the time goes:
time: 1240 us; the launch traced here: 1230 us
  starting transfers between devices  451 us (36%)
  waiting for transfers between devices  268 us (22%)
  local copies, waits for them, and re-layouts  199 us (16%)
  other arithmetic  157 us (13%)
  blocking collectives  80.2 us (6%)
  matrix products  58.8 us (5%)
  between operations  15.4 us (1%)
    ppermute x8, starting transfers between devices, with_halo(): lax.ppermute(lax.slice_in_dim(block, block.shape[dim] - width, None, axis...  374 us
    psum x1, waiting for transfers between devices, per_device(): lax.psum((grad_pradial, grad_pfilter, grad_read, grad_final, grad_aradial...  249 us
    scatter-add x11, other arithmetic, edge_backward(): grad_table = grad_table.at[indices.reshape(-1)].add(spread * filters)  130 us
    gather x19, local copies, waits for them, and re-layouts, edge_setup(): gathered = row_table[indices.reshape(-1)].astype(jnp.float32)  117 us
    psum x1, blocking collectives, per_device(): lax.psum((grad_pradial, grad_pfilter, grad_read, grad_final, grad_aradial...  80.2 us
    ppermute x8, starting transfers between devices, with_halo(): lax.ppermute(lax.slice_in_dim(block, 0, width, axis=dim), axis, backward)  77.3 us
  transfers between devices with their start and end apart: 17, of which 11 were waited for; matrix products, arithmetic and copies ran while one was open for 1% of the time, Pallas kernels for 0%

commit v1 on v0

--- a/solution.py
+++ b/solution.py
@@ -351,20 +351,23 @@
         grad_proj_probe,
         grad_gain,
     ) = lax.psum(
-        (
-            grad_pradial,
-            grad_pfilter,
-            grad_read,
-            grad_final,
-            grad_aradial,
-            grad_afilter,
-            grad_proj_input,
-            grad_mix_first,
-            grad_mix_second,
-            grad_proj_probe,
-            grad_gain,
+        lax.psum(
+            (
+                grad_pradial,
+                grad_pfilter,
+                grad_read,
+                grad_final,
+                grad_aradial,
+                grad_afilter,
+                grad_proj_input,
+                grad_mix_first,
+                grad_mix_second,
+                grad_proj_probe,
+                grad_gain,
+            ),
+            "rep",
         ),
-        ("rep", "gx", "gy"),
+        ("gx", "gy"),
     )
     grad_square = jnp.stack(
         [

time: 1240 us -> 1360 us (1.097)
  blocking collectives: 80.2 us -> 259 us
  waiting for transfers between devices: 268 us -> 205 us
    psum x1, waiting for transfers between devices: 249 us -> 0.01 us  [per_device(): lax.psum((grad_pradial, grad_pfilter, grad_read, grad_final, grad_aradial...]
    psum x0 -> x1, blocking collectives: none -> 246 us  [per_device(): lax.psum(lax.psum((grad_pradial, grad_pfilter, grad_read, grad_final, gra...]
    psum x0 -> x1, waiting for transfers between devices: none -> 183 us  [per_device(): lax.psum(lax.psum((grad_pradial, grad_pfilter, grad_read, grad_final, gra...]
    psum x1, blocking collectives: 80.2 us -> 13.3 us  [per_device(): lax.psum((grad_pradial, grad_pfilter, grad_read, grad_final, grad_aradial...]
  transfers between devices with their start and end apart: 17 -> 18, of which waited for: 11 -> 12; matrix products, arithmetic and copies ran while one was open for 1% -> 1% of each run, Pallas kernels for 0% -> 0%
where the time goes in v1:
time: 1360 us; the launch traced here: 1350 us
  starting transfers between devices  451 us (33%)
  blocking collectives  259 us (19%)
  waiting for transfers between devices  205 us (15%)
  local copies, waits for them, and re-layouts  200 us (15%)
  other arithmetic  157 us (12%)
  matrix products  58.8 us (4%)
  between operations  15.5 us (1%)
    ppermute x8, starting transfers between devices, with_halo(): lax.ppermute(lax.slice_in_dim(block, block.shape[dim] - width, None, axis...  374 us
    psum x1, blocking collectives, per_device(): lax.psum(lax.psum((grad_pradial, grad_pfilter, grad_read, grad_final, gra...  246 us
    psum x1, waiting for transfers between devices, per_device(): lax.psum(lax.psum((grad_pradial, grad_pfilter, grad_read, grad_final, gra...  183 us
    scatter-add x11, other arithmetic, edge_backward(): grad_table = grad_table.at[indices.reshape(-1)].add(spread * filters)  130 us
    gather x19, local copies, waits for them, and re-layouts, edge_setup(): gathered = row_table[indices.reshape(-1)].astype(jnp.float32)  117 us
    ppermute x8, starting transfers between devices, with_halo(): lax.ppermute(lax.slice_in_dim(block, 0, width, axis=dim), axis, backward)  77.3 us
  transfers between devices with their start and end apart: 18, of which 12 were waited for; matrix products, arithmetic and copies ran while one was open for 1% of the time, Pallas kernels for 0%

profile of v1, /device:TPU:1, one launch (start us, length us, event | category | flops | bytes accessed | tf_op | source)
XLA Modules:
  0.0 1348.0 jit_solution(15260971080371321895)
XLA Ops:
  9.6 3.2 gather_fusion.3
  15.3 4.0 collective-permute-start.1
  30.0 67.8 %while.50 = (s32[]{:T(128)}, bf16[8,64,128]{2,1,0:T(8,128)(2,1)S(1)}, s32[8,64,32]{2,1,0:T(8,128)S(1)}, bf16[1536,128]{1,0:T(8,128)(2,1)S(1)}, f32[8,64,32]{2,1,...) while((s32[]{:T(128)}, ...), condition=%wide.region_2.3_spmd, body=%wide.region_0.2_spmd.sunk | while | flops 80953368 | bytes 1840393 | solution.py:97
  31.1 6.2 gather_fusion
  39.6 6.2 gather_fusion
  48.0 6.2 gather_fusion
  56.5 6.2 gather_fusion
  65.0 6.2 gather_fusion
  73.5 6.2 gather_fusion
  81.9 6.2 gather_fusion
  90.4 6.2 gather_fusion
  100.1 3.2 gather_fusion.4
  103.5 2.9 collective-permute-start.5
  106.5 2.8 collective-permute-done.4
  117.4 99.2 %while.51 = (s32[]{:T(128)}, f32[1536,128]{1,0:T(8,128)S(1)}, f32[20,128]{1,0:T(8,128)}, f32[128,128]{1,0:T(8,128)}, f32[128,128]{1,0:T(8,128)}, /*index=5*/f32[...) while((s32[]{:T(128)}, f32[1536,128]{1,0:T(8,128)S(1)}, ...), condition=%wide.region_7.8_spmd, body=%wide.region_3.7_spmd.sunk | while | flops 237339360 | bytes 26602296 | solution.py:321
  120.2 6.2 gather_fusion.1
  136.8 11.8 scatter_fusion
  153.2 6.2 gather_fusion.1
  169.8 11.8 scatter_fusion
  186.3 6.2 gather_fusion.1
  202.9 11.8 scatter_fusion
  216.8 35.9 %collective-permute-start.8 = (bf16[1,3,128,128]{3,2,1,0:T(8,128)(2,1)S(1)}, bf16[1,3,128,128]{3,2,1,0:T(8,128)(2,1)S(1)}, u32[]{:S(2)}, u32[]{:S(2)}) collective-permute-start(bf16[1,3,128,128]{3,2,1,0:T(8,128)(2,1)S(1)} %bitcast.220), channel_id=1, source_target_pairs={{0,8},{8,16},{16,24},{24,32},{32,40},{40,48},{48,56},{56,0},{1,9},... | collective-permute-start | bytes 294920 | tf_op jit(solution)/shard_map/ppermute | solution.py:16
  252.6 66.7 %collective-permute-start.9 = (bf16[1,3,128,128]{3,2,1,0:T(8,128)(2,1)S(1)}, bf16[1,3,128,128]{3,2,1,0:T(8,128)(2,1)S(1)}, u32[]{:S(2)}, u32[]{:S(2)}) collective-permute-start(bf16[1,3,128,128]{3,2,1,0:T(8,128)(2,1)S(1)} %bitcast.218), channel_id=1, source_target_pairs={{8,0},{16,8},{24,16},{32,24},{40,32},{48,40},{56,48},{0,56},{9,1},... | collective-permute-start | bytes 294920 | tf_op jit(solution)/shard_map/ppermute | solution.py:19
  322.9 331.3 %collective-permute-start.10 = (bf16[5,1,128,128]{3,2,1,0:T(8,128)(2,1)S(1)}, bf16[5,1,128,128]{3,2,1,0:T(8,128)(2,1)S(1)}, u32[]{:S(2)}, u32[]{:S(2)}) collective-permute-start(bf16[5,1,128,128]{3,2,1,0:T(8,128)(2,1)S(1)} %get-tuple-element.649), channel_id=1, source_target_pairs={{0,1},{1,2},{2,3},{3,4},{4,5},{5,6},{6,7},{7,0},{8,9},{9,10},{10,1... | collective-permute-start | bytes 491528 | tf_op jit(solution)/shard_map/ppermute | solution.py:16
  656.5 2.8 collective-permute-done.11
  659.6 6.4 scatter_fusion.2
  669.4 197.2 %while.52 = (s32[]{:T(128)}, f32[1536,128]{1,0:T(8,128)S(1)}, f32[20,128]{1,0:T(8,128)S(1)}, f32[128,128]{1,0:T(8,128)}, s32[8,64,32]{2,1,0:T(8,128)}, /*index=5...) while((s32[]{:T(128)}, f32[1536,128]{1,0:T(8,128)S(1)}, ...), condition=%wide.region_11.12_spmd.clone, body=%wide.region_9.11_spmd.clone.sunk | while | flops 230102048 | bytes 15238644 | solution.py:123
  673.4 11.8 scatter_fusion.1
  685.2 6.2 gather_fusion.2
  698.0 11.8 scatter_fusion.1
  709.8 6.2 gather_fusion.2
  722.7 11.8 scatter_fusion.1
  734.5 6.2 gather_fusion.2
  747.3 11.8 scatter_fusion.1
  759.1 6.2 gather_fusion.2
  772.0 11.8 scatter_fusion.1
  783.8 6.2 gather_fusion.2
  796.6 11.8 scatter_fusion.1
  808.4 6.2 gather_fusion.2
  821.2 11.8 scatter_fusion.1
  833.0 6.2 gather_fusion.2
  845.9 11.8 scatter_fusion.1
  857.7 6.2 gather_fusion.2
  878.3 2.8 collective-permute-done.15
  881.4 6.1 scatter_fusion.3
  891.2 13.3 all-reduce.2
  904.5 245.6 %all-reduce = (f32[1,20,128]{2,1,0:T(8,128)S(1)}, f32[1,20,128]{2,1,0:T(8,128)S(1)}, f32[3,128]{1,0:T(4,128)S(1)}, f32[1,128]{1,0:T(1,128)S(1)}) all-reduce(f32[1,20,128]{2,1,0:T(8,128)S(1)} %bitcast.231, f32[1,20,128]{2,1,0:T(8,128)S(1)} %bitcast.232, ...), channel_id=1, replica_groups=mesh['rep'=4,'gx'=8,'gy'=8] {'gx','gy'}, use_global_device_ids=true, to_apply=%region_30.31 | all-reduce | flops 5632 | bytes 45056 | tf_op jit(solution)/shard_map/psum | solution.py:353
  1152.1 183.2 %all-reduce.7.cloned.1.call-done = (f32[1,128,128]{2,1,0:T(8,128)}, f32[1,128,128]{2,1,0:T(8,128)}, f32[1,128,128]{2,1,0:T(8,128)}, f32[1,128,128]{2,1,0:T(8,128...) async-done(((f32[1,128,128]{2,1,0:T(8,128)}, f32[1,128,128]{2,1,0:T(8,128)}, f32[1,128,128]{2,1,0:T(8,128)}, f32[1,128,128]{2,1,0:T(8,128)}, ...) | async-done | bytes 458768 | tf_op jit(solution)/shard_map/psum | solution.py:353
  (646 shorter events, 173.2 us)
Async XLA Ops:
  7.2 92.8 %copy-start = (bf16[128,128]{1,0:T(8,128)(2,1)S(1)}, bf16[128,128]{1,0:T(8,128)(2,1)}, u32[]{:S(2)}) copy-start(bf16[128,128]{1,0:T(8,128)(2,1)} %param.43) | copy-start | bytes 98308
  7.2 1144.1 %all-reduce.9.cloned.1.call-start = ((), (), s32[]{:S(2)}) async-start(), calls=%async_computation.1 | async-start | bytes 917504 | tf_op jit(solution)/shard_map/psum | solution.py:354
  12.8 9.2 collective-permute-start
  15.3 6.6 collective-permute-start.1
  19.5 87.0 %copy-start.59 = (bf16[9]{0:T(256)(128)(2,1)}, bf16[9]{0:T(256)(128)(2,1)S(1)}, u32[]{:S(2)}) copy-start(bf16[9]{0:T(256)(128)(2,1)S(1)} %pad.58.clone) | copy-start | bytes 58
  19.5 1.5 copy-start.39
  22.0 4.5 collective-permute-start.2
  24.3 4.7 collective-permute-start.3
  30.0 67.8 %copy-start.37 = (bf16[128,128]{1,0:T(8,128)(2,1)S(1)}, bf16[128,128]{1,0:T(8,128)(2,1)}, u32[]{:S(2)}) copy-start(bf16[128,128]{1,0:T(8,128)(2,1)} %param.41) | copy-start | bytes 98308
  103.4 6.0 collective-permute-start.4
  103.5 5.9 collective-permute-start.5
  109.4 1.5 copy-start.33
  109.4 3.5 collective-permute-start.6
  109.6 5.0 collective-permute-start.7
  119.2 7.2 copy-start.3
  129.4 1.6 copy-start.24
  132.5 1.7 copy-start.5
  134.2 2.5 copy-start.23
  136.8 11.8 copy-start.50
  152.3 7.2 copy-start.3
  162.5 1.6 copy-start.24
  165.6 1.7 copy-start.5
  167.3 2.6 copy-start.23
  169.8 11.8 copy-start.50
  185.4 7.2 copy-start.3
  195.5 1.6 copy-start.24
  198.7 1.7 copy-start.5
  200.3 2.6 copy-start.23
  202.9 11.8 copy-start.50
  216.8 104.5 %collective-permute-start.8 = (bf16[1,3,128,128]{3,2,1,0:T(8,128)(2,1)S(1)}, bf16[1,3,128,128]{3,2,1,0:T(8,128)(2,1)S(1)}, u32[]{:S(2)}, u32[]{:S(2)}) collective-permute-start(bf16[1,3,128,128]{3,2,1,0:T(8,128)(2,1)S(1)} %bitcast.220), channel_id=1, source_target_pairs={{0,8},{8,16},{16,24},{24,32},{32,40},{40,48},{48,56},{56,0},{1,9},... | collective-permute-start | bytes 294920 | tf_op jit(solution)/shard_map/ppermute | solution.py:16
  252.6 70.2 %collective-permute-start.9 = (bf16[1,3,128,128]{3,2,1,0:T(8,128)(2,1)S(1)}, bf16[1,3,128,128]{3,2,1,0:T(8,128)(2,1)S(1)}, u32[]{:S(2)}, u32[]{:S(2)}) collective-permute-start(bf16[1,3,128,128]{3,2,1,0:T(8,128)(2,1)S(1)} %bitcast.218), channel_id=1, source_target_pairs={{8,0},{16,8},{24,16},{32,24},{40,32},{48,40},{56,48},{0,56},{9,1},... | collective-permute-start | bytes 294920 | tf_op jit(solution)/shard_map/ppermute | solution.py:19
  322.9 331.4 %copy-start.52 = (s32[1,1,1,8,128]{4,3,2,1,0:T(8,128)S(1)}, s32[1,1,1,8,128]{4,3,2,1,0:T(8,128)}, u32[]{:S(2)}) copy-start(s32[1,1,1,8,128]{4,3,2,1,0:T(8,128)} %param.32) | copy-start | bytes 12292
  322.9 333.6 %collective-permute-start.10 = (bf16[5,1,128,128]{3,2,1,0:T(8,128)(2,1)S(1)}, bf16[5,1,128,128]{3,2,1,0:T(8,128)(2,1)S(1)}, u32[]{:S(2)}, u32[]{:S(2)}) collective-permute-start(bf16[5,1,128,128]{3,2,1,0:T(8,128)(2,1)S(1)} %get-tuple-element.649), channel_id=1, source_target_pairs={{0,1},{1,2},{2,3},{3,4},{4,5},{5,6},{6,7},{7,0},{8,9},{9,10},{10,1... | collective-permute-start | bytes 491528 | tf_op jit(solution)/shard_map/ppermute | solution.py:16
  654.2 5.0 collective-permute-start.11
  692.6 1.4 copy-start.10
  717.2 1.4 copy-start.10
  741.9 1.4 copy-start.10
  766.5 1.4 copy-start.10
  791.1 1.4 copy-start.10
  840.4 1.4 copy-start.10
  869.4 4.7 collective-permute-start.12
  869.4 4.7 collective-permute-start.13
  874.1 2.2 copy-start.19
  874.1 2.2 copy-start.21
  874.2 4.1 collective-permute-start.14
  876.0 5.0 collective-permute-start.15
  881.4 6.2 copy-start.36
  889.4 445.9 %all-reduce.7.cloned.1.call-start = ((), (), s32[]{:S(2)}) async-start(), calls=%async_computation | async-start | bytes 917504 | tf_op jit(solution)/shard_map/psum | solution.py:353
  (101 other events, 86.5 us)
Sparse Core Ops, SparseCore 0:
  889.5 47.6 all-reduce.8
  1151.4 183.8 all-reduce.6
